TPU v7x, 512 devices: a whole 4x8x8 slice. The times are simulated.
512 devices in a mesh: expert: 64 (over x, z, core), group: 8 (over y).
Axes of the slice: x: 4, y: 8, z: 8, core: 2. Of those that a mesh axis runs over, the one named last changes fastest.
Arguments:
- tokens: bfloat16 [4096, 4096], P('expert', 'group'), may hold values from -6 to 6
- gate_weight: bfloat16 [64, 1536, 4096], P('expert', 'group'), may hold values from -0.09375 to 0.09375
- up_weight: bfloat16 [64, 1536, 4096], P('expert', 'group'), may hold values from -0.09375 to 0.09375
- down_weight: bfloat16 [64, 1536, 4096], P('expert', 'group'), may hold values from -0.15625 to 0.15625
- expert_ids: int32 [4096, 8], P('expert'), may hold values from 0 to 63, all different within a row; in each aligned block of 64 rows (0 to 63, 64 to 127, ...) at most 12 rows name the same one
- gate_scores: bfloat16 [4096, 8], P('expert'), may hold values from 0.19921875 to 1
Outputs:
- mixed: bfloat16 [4096, 4096], P('expert', 'group')
Inputs may be any that keep to these rules, and one draw needn't show every extreme that they name: `expert_ids`: the 8 experts of a token are distinct; within the 64 rows of one device no expert is named by more than 12 rows, a bound that some block reaches.
All inputs are finite; a program needn't handle non-finite values.
Results may differ from a plain program's by a relative error of at most 0.019.
Values may be sent and summed in bfloat16 or wider, within the bound.
No kernel may reach another device: no remote copies, remote signals or barrier semaphores. Data moves between devices by JAX's collectives and lax.ppermute only.
A program may use at most 128 MiB of HBM per device.

v0:
```python
import jax
import jax.numpy as jnp
from jax import lax
from jax.sharding import PartitionSpec as P


def route_tables(expert_ids, gate_scores, experts):
    tok_rows, top_count = expert_ids.shape
    capacity = tok_rows * top_count * 3 // (2 * experts)
    flat_ids = expert_ids.reshape(-1)
    onehot = (flat_ids[:, None] == jnp.arange(experts, dtype=jnp.int32)[None, :]).astype(jnp.int32)
    before = jnp.cumsum(onehot, axis=0) - onehot
    slot_index = jnp.sum(before * onehot, axis=1).reshape(tok_rows, top_count)
    slot_keys = expert_ids * capacity + slot_index
    columns = jnp.arange(experts * capacity, dtype=jnp.int32)
    matches = slot_keys[:, :, None] == columns[None, None, :]
    selector = jnp.any(matches, axis=1).astype(jnp.bfloat16)
    weights = jnp.sum(
        jnp.where(matches, gate_scores[:, :, None].astype(jnp.float32), 0.0), axis=1
    ).astype(jnp.bfloat16)
    return capacity, selector, weights


def transposed_down(w):
    groups = lax.axis_size("group")
    me = lax.axis_index("group")
    width = w.shape[1] // groups
    received = [lax.dynamic_slice_in_dim(w, me * width, width, axis=1)]
    for s in range(1, groups):
        dest = (me + groups - s) % groups
        piece = lax.dynamic_slice_in_dim(w, dest * width, width, axis=1)
        received.append(
            lax.ppermute(piece, "group", [(j, (j - s) % groups) for j in range(groups)])
        )
    stacked = jnp.stack(received)
    return jnp.roll(stacked, me, axis=0).reshape(groups * w.shape[0], width)


def layer(tokens, gate_weight, up_weight, down_weight, expert_ids, gate_scores):
    experts = lax.axis_size("expert")
    capacity, selector, weights = route_tables(expert_ids, gate_scores, experts)
    placed = lax.dot_general(
        selector, tokens, (((0,), (0,)), ((), ())), preferred_element_type=jnp.float32
    ).astype(jnp.bfloat16)
    down_cols = transposed_down(down_weight[0])
    arrived = lax.all_to_all(
        placed.reshape(experts, capacity, tokens.shape[1]), "expert", 0, 0, tiled=True
    ).reshape(experts * capacity, tokens.shape[1])
    row_block = lax.all_gather(arrived, "group", axis=1, tiled=True)

    gate_value = lax.dot_general(
        row_block, gate_weight[0], (((1,), (1,)), ((), ())), preferred_element_type=jnp.float32
    )
    up_value = lax.dot_general(
        row_block, up_weight[0], (((1,), (1,)), ((), ())), preferred_element_type=jnp.float32
    )
    hidden = (jax.nn.silu(gate_value) * up_value).astype(jnp.bfloat16)
    hidden_all = lax.all_gather(hidden, "group", axis=1, tiled=True)
    partial_value = jnp.dot(hidden_all, down_cols, preferred_element_type=jnp.float32)
    returned = lax.all_to_all(
        partial_value.astype(jnp.bfloat16).reshape(experts, capacity, -1), "expert", 0, 0, tiled=True
    ).reshape(experts * capacity, -1)
    combined = jnp.dot(weights, returned, preferred_element_type=jnp.float32)
    return combined.astype(jnp.bfloat16)


def solution(mesh):
    placed = (
        P("expert", "group"),
        P("expert", "group", None),
        P("expert", "group", None),
        P("expert", "group", None),
        P("expert", None),
        P("expert", None),
    )
    return jax.shard_map(
        layer, mesh=mesh, in_specs=placed, out_specs=P("expert", "group"), check_vma=False
    )
```

profile of v0, /device:TPU:1, one launch (start us, length us, event | category | flops | bytes accessed | tf_op | source)
XLA Modules:
  0.0 272.8 jit_solution(14634485627550809246)
XLA Ops:
  6.5 0.9 copy.21
  7.4 0.1 eq.53
  7.5 0.1 eq.49
  7.6 1.2 reduce-window.6
  8.8 0.2 slice_reduce_fusion
  9.1 0.1 fusion.13
  9.2 0.1 reshape.48
  9.3 0.1 copy.24
  9.4 0.7 multiply_add_fusion
  10.1 0.1 copy.25
  10.2 0.5 fusion.4
  10.7 0.1 copy-done.2
  10.8 1.3 convolution_convert_fusion
  12.1 0.2 reshape.49
  12.2 43.3 %all_to_all.10 = bf16[64,12,512]{2,1,0:T(8,128)(2,1)} all-to-all(bf16[64,12,512]{2,1,0:T(8,128)(2,1)S(1)} %reshape.49), channel_id=1, replica_groups=mesh['expert'=64,'group'=8] {'expert'}, dimensions={0} | all-to-all | bytes 1572864 | tf_op jit(solution)/shard_map/all_to_all | solution.py:46
  55.5 2.1 reshape.50
  57.6 0.0 all-gather.3.cloned.1.call-update
  57.6 0.0 all-gather.5.cloned.1.call-start
  57.6 73.5 %all-gather.3.cloned.1.call-done = bf16[768,4096]{1,0:T(8,128)(2,1)} async-done(((bf16[768,512]{1,0:T(8,128)(2,1)}), bf16[768,4096]{1,0:T(8,128)(2,1)}) %all-gather.3.cloned.1.call-update) | async-done | bytes 6291472 | tf_op jit(solution)/shard_map/all_gather | solution.py:49
  131.2 0.0 copy-done
  131.2 5.2 %fusion.2 = f32[768,192]{0,1:T(8,128)S(1)} fusion(bf16[768,4096]{1,0:T(8,128)(2,1)} %all-gather.3.cloned.1.call-done, bf16[1,192,4096]{2,1,0:T(8,128)(2,1)S(1)} %copy-done), kind=kOutput, calls=%fused_computation.2 | convolution fusion | flops 1207959552 | bytes 8454144 | tf_op jit(solution)/shard_map/dot_general | solution.py:51
  136.3 0.0 copy-start.1
  136.3 4.5 %fusion.8 = bf16[768,192]{0,1:T(8,128)(2,1)} fusion(bf16[768,4096]{1,0:T(8,128)(2,1)S(1)} %copy-done.5, bf16[1,192,4096]{2,1,0:T(8,128)(2,1)} %param.8, f32[768,192]{0,1:T(8,128)S(1)} %fusion.2), kind=kOutput, calls=%fused_computation.10 | convolution fusion | flops 1208844288 | bytes 8749056 | tf_op jit(solution)/shard_map/dot_general | solution.py:54
  140.8 0.0 all-gather.5.cloned.1.call-update
  141.0 1.2 dynamic-slice_bitcast_fusion
  142.2 3.0 %collective-permute-start = (bf16[192,512]{1,0:T(8,128)(2,1)}, bf16[192,512]{1,0:T(8,128)(2,1)S(1)}, u32[]{:S(2)}, u32[]{:S(2)}) collective-permute-start(bf16[192,512]{1,0:T(8,128)(2,1)} %get-tuple-element.11), channel_id=1, source_target_pairs={{0,7},{1,0},{2,1},{3,2},{4,3},{5,4},{6,5},{7,6},{8,15},{9,8},{10,9... | collective-permute-start | bytes 589832 | tf_op jit(solution)/shard_map/ppermute | solution.py:33
  145.2 3.9 %collective-permute-start.1 = (bf16[192,512]{1,0:T(8,128)(2,1)}, bf16[192,512]{1,0:T(8,128)(2,1)S(1)}, u32[]{:S(2)}, u32[]{:S(2)}) collective-permute-start(bf16[192,512]{1,0:T(8,128)(2,1)} %get-tuple-element.10), channel_id=1, source_target_pairs={{0,6},{1,7},{2,0},{3,1},{4,2},{5,3},{6,4},{7,5},{8,14},{9,15},{10,... | collective-permute-start | bytes 589832 | tf_op jit(solution)/shard_map/ppermute | solution.py:33
  149.2 4.0 %collective-permute-start.2 = (bf16[192,512]{1,0:T(8,128)(2,1)}, bf16[192,512]{1,0:T(8,128)(2,1)}, u32[]{:S(2)}, u32[]{:S(2)}) collective-permute-start(bf16[192,512]{1,0:T(8,128)(2,1)} %get-tuple-element.9), channel_id=1, source_target_pairs={{0,5},{1,6},{2,7},{3,0},{4,1},{5,2},{6,3},{7,4},{8,13},{9,14},{10,... | collective-permute-start | bytes 589832 | tf_op jit(solution)/shard_map/ppermute | solution.py:33
  153.2 4.3 %collective-permute-start.3 = (bf16[192,512]{1,0:T(8,128)(2,1)}, bf16[192,512]{1,0:T(8,128)(2,1)}, u32[]{:S(2)}, u32[]{:S(2)}) collective-permute-start(bf16[192,512]{1,0:T(8,128)(2,1)} %get-tuple-element.8), channel_id=1, source_target_pairs={{0,4},{1,5},{2,6},{3,7},{4,0},{5,1},{6,2},{7,3},{8,12},{9,13},{10,... | collective-permute-start | bytes 589832 | tf_op jit(solution)/shard_map/ppermute | solution.py:33
  157.5 2.8 %collective-permute-start.4 = (bf16[192,512]{1,0:T(8,128)(2,1)}, bf16[192,512]{1,0:T(8,128)(2,1)}, u32[]{:S(2)}, u32[]{:S(2)}) collective-permute-start(bf16[192,512]{1,0:T(8,128)(2,1)} %get-tuple-element.7), channel_id=1, source_target_pairs={{0,3},{1,4},{2,5},{3,6},{4,7},{5,0},{6,1},{7,2},{8,11},{9,12},{10,... | collective-permute-start | bytes 589832 | tf_op jit(solution)/shard_map/ppermute | solution.py:33
  160.3 0.0 collective-permute-done
  160.3 5.5 %collective-permute-start.5 = (bf16[192,512]{1,0:T(8,128)(2,1)}, bf16[192,512]{1,0:T(8,128)(2,1)S(1)}, u32[]{:S(2)}, u32[]{:S(2)}) collective-permute-start(bf16[192,512]{1,0:T(8,128)(2,1)} %get-tuple-element.12), channel_id=1, source_target_pairs={{0,2},{1,3},{2,4},{3,5},{4,6},{5,7},{6,0},{7,1},{8,10},{9,11},{10,... | collective-permute-start | bytes 589832 | tf_op jit(solution)/shard_map/ppermute | solution.py:33
  165.8 0.7 bitcast_dynamic-update-slice_fusion.12
  166.5 0.0 collective-permute-done.1
  166.5 1.9 collective-permute-start.6
  168.4 0.7 bitcast_dynamic-update-slice_fusion.10
  169.1 4.2 %collective-permute-done.2 = bf16[192,512]{1,0:T(8,128)(2,1)} collective-permute-done((bf16[192,512]{1,0:T(8,128)(2,1)}, bf16[192,512]{1,0:T(8,128)(2,1)}, u32[]{:S(2)}, u32[]{:S(2)}) %collective-permute-start.2) | collective-permute-done | bytes 196640 | tf_op jit(solution)/shard_map/ppermute | solution.py:33
  173.3 1.6 bitcast_dynamic-update-slice_fusion.8
  174.9 0.0 collective-permute-done.3
  174.9 1.6 bitcast_dynamic-update-slice_fusion.6
  176.5 10.5 %collective-permute-done.4 = bf16[192,512]{1,0:T(8,128)(2,1)} collective-permute-done((bf16[192,512]{1,0:T(8,128)(2,1)}, bf16[192,512]{1,0:T(8,128)(2,1)}, u32[]{:S(2)}, u32[]{:S(2)}) %collective-permute-start.4) | collective-permute-done | bytes 196640 | tf_op jit(solution)/shard_map/ppermute | solution.py:33
  187.1 1.6 bitcast_dynamic-update-slice_fusion.4
  188.7 12.9 %collective-permute-done.5 = bf16[192,512]{1,0:T(8,128)(2,1)S(1)} collective-permute-done((bf16[192,512]{1,0:T(8,128)(2,1)}, bf16[192,512]{1,0:T(8,128)(2,1)S(1)}, u32[]{:S(2)}, u32[]{:S(2)}) %collective-permute-start.5) | collective-permute-done | bytes 196640 | tf_op jit(solution)/shard_map/ppermute | solution.py:33
  201.6 0.7 bitcast_dynamic-update-slice_fusion.2
  202.3 6.0 %collective-permute-done.6 = bf16[192,512]{1,0:T(8,128)(2,1)S(1)} collective-permute-done((bf16[192,512]{1,0:T(8,128)(2,1)}, bf16[192,512]{1,0:T(8,128)(2,1)S(1)}, u32[]{:S(2)}, u32[]{:S(2)}) %collective-permute-start.6) | collective-permute-done | bytes 196640 | tf_op jit(solution)/shard_map/ppermute | solution.py:33
  208.3 0.7 bitcast_dynamic-update-slice_fusion
  209.0 0.7 dynamic-slice_dynamic-update-slice_fusion.1
  209.7 0.7 bitcast_dynamic-update-slice_fusion.13
  210.4 0.7 bitcast_dynamic-update-slice_fusion.11
  211.1 1.6 bitcast_dynamic-update-slice_fusion.9
  212.7 1.6 bitcast_dynamic-update-slice_fusion.7
  214.3 1.6 bitcast_dynamic-update-slice_fusion.5
  215.9 0.7 bitcast_dynamic-update-slice_fusion.3
  216.6 0.7 bitcast_dynamic-update-slice_fusion.1
  217.3 1.6 constant_dynamic-slice_fusion
  218.9 0.0 all-gather.5.cloned.1.call-done
  218.9 4.0 %convolution_convert_fusion.1 = bf16[768,512]{1,0:T(8,128)(2,1)} fusion(bf16[768,1536]{0,1:T(8,128)(2,1)} %all-gather.5.cloned.1.call-done, bf16[1536,512]{1,0:T(8,128)(2,1)S(1)} %bitcast.73), kind=kOutput, calls=%fused_computation.8 | convolution fusion | flops 1208352768 | bytes 4718592 | tf_op jit(solution)/shard_map/dot_general | solution.py:59
  222.9 2.1 reshape.52
  225.1 11.3 %all-to-all-start.1 = ((bf16[64,12,512]{2,1,0:T(8,128)(2,1)}), bf16[64,12,512]{2,1,0:T(8,128)(2,1)S(1)}, u32[]{:S(2)}, u32[]{:S(2)}) async-start(bf16[64,12,512]{2,1,0:T(8,128)(2,1)} %reshape.52), calls=%async_computation.1 | async-start | bytes 2097152 | tf_op jit(solution)/shard_map/all_to_all | solution.py:60
  236.4 0.1 copy.26
  236.5 0.6 select_reduce_fusion
  237.0 27.9 %all-to-all-done.1 = bf16[64,12,512]{2,1,0:T(8,128)(2,1)S(1)} async-done(((bf16[64,12,512]{2,1,0:T(8,128)(2,1)}), bf16[64,12,512]{2,1,0:T(8,128)(2,1)S(1)}, u32[]{:S(2)}, u32[]{:S(2)}) %all-to-all-start.1) | async-done | bytes 786464 | tf_op jit(solution)/shard_map/all_to_all | solution.py:60
  264.9 0.2 reshape.53
  265.1 0.9 convolution_convert_fusion.2
  (13 shorter events, 0.1 us)
Async XLA Ops:
  6.5 124.6 %copy-start = (bf16[1,192,4096]{2,1,0:T(8,128)(2,1)S(1)}, bf16[1,192,4096]{2,1,0:T(8,128)(2,1)}, u32[]{:S(2)}) copy-start(bf16[1,192,4096]{2,1,0:T(8,128)(2,1)} %param.7) | copy-start | bytes 4718596
  6.5 124.6 %all-gather.3.cloned.1.call-start = ((), (), s32[]{:S(2)}) async-start(), calls=%async_computation.2 | async-start | bytes 7077888 | tf_op jit(solution)/shard_map/all_gather | solution.py:49
  10.2 0.6 copy-start.2
  57.6 161.3 %all-gather.5.cloned.1.call-start = ((), (), s32[]{:S(2)}) async-start(), calls=%async_computation.3 | async-start | bytes 2654208 | tf_op jit(solution)/shard_map/all_gather | solution.py:58
  131.2 5.2 %copy-start.5 = (bf16[768,4096]{1,0:T(8,128)(2,1)S(1)}, bf16[768,4096]{1,0:T(8,128)(2,1)}, u32[]{:S(2)}) copy-start(bf16[768,4096]{1,0:T(8,128)(2,1)} %all-gather.3.cloned.1.call-done) | copy-start | bytes 18874372
  136.3 4.6 %copy-start.1 = (bf16[1,192,4096]{2,1,0:T(8,128)(2,1)S(1)}, bf16[1,192,4096]{2,1,0:T(8,128)(2,1)}, u32[]{:S(2)}) copy-start(bf16[1,192,4096]{2,1,0:T(8,128)(2,1)} %param.9) | copy-start | bytes 4718596
  142.2 18.1 %collective-permute-start = (bf16[192,512]{1,0:T(8,128)(2,1)}, bf16[192,512]{1,0:T(8,128)(2,1)S(1)}, u32[]{:S(2)}, u32[]{:S(2)}) collective-permute-start(bf16[192,512]{1,0:T(8,128)(2,1)} %get-tuple-element.11), channel_id=1, source_target_pairs={{0,7},{1,0},{2,1},{3,2},{4,3},{5,4},{6,5},{7,6},{8,15},{9,8},{10,9... | collective-permute-start | bytes 589832 | tf_op jit(solution)/shard_map/ppermute | solution.py:33
  145.2 21.3 %collective-permute-start.1 = (bf16[192,512]{1,0:T(8,128)(2,1)}, bf16[192,512]{1,0:T(8,128)(2,1)S(1)}, u32[]{:S(2)}, u32[]{:S(2)}) collective-permute-start(bf16[192,512]{1,0:T(8,128)(2,1)} %get-tuple-element.10), channel_id=1, source_target_pairs={{0,6},{1,7},{2,0},{3,1},{4,2},{5,3},{6,4},{7,5},{8,14},{9,15},{10,... | collective-permute-start | bytes 589832 | tf_op jit(solution)/shard_map/ppermute | solution.py:33
  149.2 24.1 %collective-permute-start.2 = (bf16[192,512]{1,0:T(8,128)(2,1)}, bf16[192,512]{1,0:T(8,128)(2,1)}, u32[]{:S(2)}, u32[]{:S(2)}) collective-permute-start(bf16[192,512]{1,0:T(8,128)(2,1)} %get-tuple-element.9), channel_id=1, source_target_pairs={{0,5},{1,6},{2,7},{3,0},{4,1},{5,2},{6,3},{7,4},{8,13},{9,14},{10,... | collective-permute-start | bytes 589832 | tf_op jit(solution)/shard_map/ppermute | solution.py:33
  153.2 21.7 %collective-permute-start.3 = (bf16[192,512]{1,0:T(8,128)(2,1)}, bf16[192,512]{1,0:T(8,128)(2,1)}, u32[]{:S(2)}, u32[]{:S(2)}) collective-permute-start(bf16[192,512]{1,0:T(8,128)(2,1)} %get-tuple-element.8), channel_id=1, source_target_pairs={{0,4},{1,5},{2,6},{3,7},{4,0},{5,1},{6,2},{7,3},{8,12},{9,13},{10,... | collective-permute-start | bytes 589832 | tf_op jit(solution)/shard_map/ppermute | solution.py:33
  157.5 29.6 %collective-permute-start.4 = (bf16[192,512]{1,0:T(8,128)(2,1)}, bf16[192,512]{1,0:T(8,128)(2,1)}, u32[]{:S(2)}, u32[]{:S(2)}) collective-permute-start(bf16[192,512]{1,0:T(8,128)(2,1)} %get-tuple-element.7), channel_id=1, source_target_pairs={{0,3},{1,4},{2,5},{3,6},{4,7},{5,0},{6,1},{7,2},{8,11},{9,12},{10,... | collective-permute-start | bytes 589832 | tf_op jit(solution)/shard_map/ppermute | solution.py:33
  160.3 41.3 %collective-permute-start.5 = (bf16[192,512]{1,0:T(8,128)(2,1)}, bf16[192,512]{1,0:T(8,128)(2,1)S(1)}, u32[]{:S(2)}, u32[]{:S(2)}) collective-permute-start(bf16[192,512]{1,0:T(8,128)(2,1)} %get-tuple-element.12), channel_id=1, source_target_pairs={{0,2},{1,3},{2,4},{3,5},{4,6},{5,7},{6,0},{7,1},{8,10},{9,11},{10,... | collective-permute-start | bytes 589832 | tf_op jit(solution)/shard_map/ppermute | solution.py:33
  166.5 41.8 %collective-permute-start.6 = (bf16[192,512]{1,0:T(8,128)(2,1)}, bf16[192,512]{1,0:T(8,128)(2,1)S(1)}, u32[]{:S(2)}, u32[]{:S(2)}) collective-permute-start(bf16[192,512]{1,0:T(8,128)(2,1)} %get-tuple-element.5), channel_id=1, source_target_pairs={{0,1},{1,2},{2,3},{3,4},{4,5},{5,6},{6,7},{7,0},{8,9},{9,10},{10,1... | collective-permute-start | bytes 589832 | tf_op jit(solution)/shard_map/ppermute | solution.py:33
  222.9 13.4 %copy-start.4 = (bf16[64,8]{0,1:T(8,128)(2,1)S(1)}, bf16[64,8]{0,1:T(8,128)(2,1)}, u32[]{:S(2)}) copy-start(bf16[64,8]{0,1:T(8,128)(2,1)} %param.11) | copy-start | bytes 3076
  222.9 13.5 %copy-start.3 = (s32[64,8]{1,0:T(8,128)S(1)}, s32[64,8]{1,0:T(8,128)}, u32[]{:S(2)}) copy-start(s32[64,8]{1,0:T(8,128)} %copy-done.2) | copy-start | bytes 6148
  225.1 39.8 %all-to-all-start.1 = ((bf16[64,12,512]{2,1,0:T(8,128)(2,1)}), bf16[64,12,512]{2,1,0:T(8,128)(2,1)S(1)}, u32[]{:S(2)}, u32[]{:S(2)}) async-start(bf16[64,12,512]{2,1,0:T(8,128)(2,1)} %reshape.52), calls=%async_computation.1 | async-start | bytes 2097152 | tf_op jit(solution)/shard_map/all_to_all | solution.py:60
Sparse Core Ops, SparseCore 0:
  57.7 73.4 all-gather.2
  141.0 71.8 all-gather.4
where the time goes:
time: 274 us; the launch traced here: 273 us
  waiting for transfers between devices  135 us (49%)
  blocking collectives  43.3 us (16%)
  starting transfers between devices  36.8 us (13%)
  local copies, waits for them, and re-layouts  25 us (9%)
  matrix products  15.8 us (6%)
  between operations  13.7 us (5%)
  other arithmetic  3.17 us (1%)
    all_gather x1, waiting for transfers between devices, layer(): row_block = lax.all_gather(arrived, 'group', axis=1, tiled=True)  73.5 us
    all_to_all x1, blocking collectives, layer(): lax.all_to_all(placed.reshape(experts, capacity, tokens.shape[1]), 'exper...  43.3 us
    ppermute x7, waiting for transfers between devices, transposed_down(): lax.ppermute(piece, 'group', [(j, (j - s) % groups) for j in range(groups)])  33.6 us
    all_to_all x1, waiting for transfers between devices, layer(): lax.all_to_all(partial_value.astype(jnp.bfloat16).reshape(experts, capaci...  27.9 us
    ppermute x7, starting transfers between devices, transposed_down(): lax.ppermute(piece, 'group', [(j, (j - s) % groups) for j in range(groups)])  25.5 us
    unnamed x27, local copies, waits for them, and re-layouts  16.3 us
    all_to_all x1, starting transfers between devices, layer(): lax.all_to_all(partial_value.astype(jnp.bfloat16).reshape(experts, capaci...  11.3 us
  transfers between devices with their start and end apart: 10, of which 6 were waited for; matrix products, arithmetic and copies ran while one was open for 7% of the time, Pallas kernels for 0%

commit v1 on v0

--- a/solution.py
+++ b/solution.py
@@ -25,15 +25,14 @@
     groups = lax.axis_size("group")
     me = lax.axis_index("group")
     width = w.shape[1] // groups
-    received = [lax.dynamic_slice_in_dim(w, me * width, width, axis=1)]
+    by_dest = jnp.roll(w.reshape(w.shape[0], groups, width), -me, axis=1)
+    received = [by_dest[:, 0]]
     for s in range(1, groups):
-        dest = (me + groups - s) % groups
-        piece = lax.dynamic_slice_in_dim(w, dest * width, width, axis=1)
+        piece = by_dest[:, groups - s]
         received.append(
             lax.ppermute(piece, "group", [(j, (j - s) % groups) for j in range(groups)])
         )
-    stacked = jnp.stack(received)
-    return jnp.roll(stacked, me, axis=0).reshape(groups * w.shape[0], width)
+    return jnp.concatenate(received, axis=0)
 
 
 def layer(tokens, gate_weight, up_weight, down_weight, expert_ids, gate_scores):
@@ -56,6 +55,10 @@
     )
     hidden = (jax.nn.silu(gate_value) * up_value).astype(jnp.bfloat16)
     hidden_all = lax.all_gather(hidden, "group", axis=1, tiled=True)
+    groups = lax.axis_size("group")
+    hidden_all = jnp.roll(
+        hidden_all.reshape(hidden.shape[0], groups, hidden.shape[1]), -lax.axis_index("group"), axis=1
+    ).reshape(hidden.shape[0], -1)
     partial_value = jnp.dot(hidden_all, down_cols, preferred_element_type=jnp.float32)
     returned = lax.all_to_all(
         partial_value.astype(jnp.bfloat16).reshape(experts, capacity, -1), "expert", 0, 0, tiled=True
@@ -73,6 +76,4 @@
         P("expert", None),
         P("expert", None),
     )
-    return jax.shard_map(
-        layer, mesh=mesh, in_specs=placed, out_specs=P("expert", "group"), check_vma=False
-    )
+    return jax.shard_map(layer, mesh=mesh, in_specs=placed, out_specs=P("expert", "group"), check_vma=False)

time: 274 us -> 269 us (0.982)
  local copies, waits for them, and re-layouts: 25 us -> 15.9 us
  other arithmetic: 3.17 us -> 6.76 us
  waiting for transfers between devices: 135 us -> 138 us
    unnamed x27 -> x24, local copies, waits for them, and re-layouts: 16.3 us -> 8.02 us
    concatenate x0 -> x2, other arithmetic: none -> 3.59 us  [the longest x1 2.51 us: layer(): jnp.roll(hidden_all.reshape(hidden.shape[0], groups, hidden.shape[1]), -l...]
    slice x1 -> x2, local copies, waits for them, and re-layouts: 0.23 us -> 3.11 us  [the longest x1 2.88 us: transposed_down(): piece = by_dest[:, groups - s]]
    dynamic_slice x2 -> x0, local copies, waits for them, and re-layouts: 2.77 us -> none  [the longest x1 1.57 us: transposed_down(): return jnp.roll(stacked, me, axis=0).reshape(groups * w.shape[0], width)]
  transfers between devices with their start and end apart: 10 -> 10, of which waited for: 6 -> 7; matrix products, arithmetic and copies ran while one was open for 7% -> 5% of each run, Pallas kernels for 0% -> 0%
where the time goes in v1:
time: 269 us; the launch traced here: 268 us
  waiting for transfers between devices  138 us (51%)
  blocking collectives  43.3 us (16%)
  starting transfers between devices  37.1 us (14%)
  local copies, waits for them, and re-layouts  15.9 us (6%)
  between operations  13.7 us (5%)
  matrix products  13.1 us (5%)
  other arithmetic  6.76 us (3%)
    all_gather x1, waiting for transfers between devices, layer(): row_block = lax.all_gather(arrived, 'group', axis=1, tiled=True)  73.5 us
    all_to_all x1, blocking collectives, layer(): lax.all_to_all(placed.reshape(experts, capacity, tokens.shape[1]), 'exper...  43.3 us
    ppermute x7, waiting for transfers between devices, transposed_down(): lax.ppermute(piece, 'group', [(j, (j - s) % groups) for j in range(groups)])  34.4 us
    all_to_all x1, waiting for transfers between devices, layer(): lax.all_to_all(partial_value.astype(jnp.bfloat16).reshape(experts, capaci...  27.9 us
    ppermute x7, starting transfers between devices, transposed_down(): lax.ppermute(piece, 'group', [(j, (j - s) % groups) for j in range(groups)])  25.7 us
    all_to_all x1, starting transfers between devices, layer(): lax.all_to_all(partial_value.astype(jnp.bfloat16).reshape(experts, capaci...  11.4 us
    unnamed x24, local copies, waits for them, and re-layouts  8.02 us
  transfers between devices with their start and end apart: 10, of which 7 were waited for; matrix products, arithmetic and copies ran while one was open for 5% of the time, Pallas kernels for 0%

profile of v1, /device:TPU:1, one launch (start us, length us, event | category | flops | bytes accessed | tf_op | source)
XLA Modules:
  0.0 268.2 jit_solution(1106308977775681720)
XLA Ops:
  6.5 0.0 copy-start
  6.5 0.0 all-gather.3.cloned.1.call-start
  6.5 0.9 copy.97
  7.4 0.1 eq.47
  7.5 0.1 eq.43
  7.6 1.2 reduce-window.6
  8.8 0.2 slice_reduce_fusion
  9.1 0.1 fusion.15
  9.2 0.1 reshape.42
  9.3 0.1 copy.100
  9.4 0.7 multiply_add_fusion
  10.1 0.1 copy.101
  10.2 0.5 fusion.6
  10.7 1.3 convolution_convert_fusion
  12.0 0.2 reshape.43
  12.2 43.3 %all_to_all.10 = bf16[64,12,512]{2,1,0:T(8,128)(2,1)} all-to-all(bf16[64,12,512]{2,1,0:T(8,128)(2,1)S(1)} %reshape.43), channel_id=1, replica_groups=mesh['expert'=64,'group'=8] {'expert'}, dimensions={0} | all-to-all | bytes 1572864 | tf_op jit(solution)/shard_map/all_to_all | solution.py:45
  55.4 2.1 reshape.44
  57.5 0.0 all-gather.3.cloned.1.call-update
  57.5 0.0 copy-start.3
  57.5 0.0 all-gather.5.cloned.1.call-start
  57.6 73.5 %all-gather.3.cloned.1.call-done = bf16[768,4096]{1,0:T(8,128)(2,1)} async-done(((bf16[768,512]{1,0:T(8,128)(2,1)}), bf16[768,4096]{1,0:T(8,128)(2,1)}) %all-gather.3.cloned.1.call-update) | async-done | bytes 6291472 | tf_op jit(solution)/shard_map/all_gather | solution.py:48
  131.1 0.0 copy-done
  131.1 5.1 %fusion.4 = f32[768,192]{0,1:T(8,128)S(1)} fusion(bf16[768,4096]{1,0:T(8,128)(2,1)} %all-gather.3.cloned.1.call-done, bf16[1,192,4096]{2,1,0:T(8,128)(2,1)S(1)} %copy-done), kind=kOutput, calls=%fused_computation.8 | convolution fusion | flops 1207959552 | bytes 8454144 | tf_op jit(solution)/shard_map/dot_general | solution.py:50
  136.2 0.0 copy-done.3
  136.3 0.0 copy-done.2
  136.3 3.0 %fusion.10 = bf16[768,192]{0,1:T(8,128)(2,1)} fusion(bf16[768,4096]{1,0:T(8,128)(2,1)S(1)} %copy-done.2, bf16[1,192,4096]{2,1,0:T(8,128)(2,1)S(1)} %copy-done.3, f32[768,192]{0,1:T(8,128)S(1)} %fusion.4), kind=kOutput, calls=%fused_computation.16 | convolution fusion | flops 1208844288 | bytes 8749056 | tf_op jit(solution)/shard_map/dot_general | solution.py:53
  139.2 0.0 all-gather.5.cloned.1.call-update
  139.3 2.1 copy.112
  141.3 1.1 fusion.1
  142.4 2.9 %fusion.18 = (bf16[192,1,512]{2,1,0:T(2,128)(2,1)S(1)}, bf16[192,1,512]{2,1,0:T(2,128)(2,1)S(1)}, bf16[192,1,512]{2,1,0:T(2,128)(2,1)S(1)}, bf16[192,1,512]{2,1,...) fusion(bf16[192,8,512]{2,1,0:T(8,128)(2,1)S(1)} %fusion.1), kind=kLoop, calls=%fused_computation.44 | loop fusion | bytes 3145728 | tf_op jit(solution)/shard_map/slice | solution.py:31
  145.3 3.1 %collective-permute-start = (bf16[192,512]{1,0:T(8,128)(2,1)S(1)}, bf16[192,512]{1,0:T(8,128)(2,1)S(1)}, u32[]{:S(2)}, u32[]{:S(2)}) collective-permute-start(bf16[192,512]{1,0:T(8,128)(2,1)S(1)} %bitcast.75), channel_id=1, source_target_pairs={{0,7},{1,0},{2,1},{3,2},{4,3},{5,4},{6,5},{7,6},{8,15},{9,8},{10,9... | collective-permute-start | bytes 589832 | tf_op jit(solution)/shard_map/ppermute | solution.py:33
  148.5 3.9 %collective-permute-start.1 = (bf16[192,512]{1,0:T(8,128)(2,1)S(1)}, bf16[192,512]{1,0:T(8,128)(2,1)S(1)}, u32[]{:S(2)}, u32[]{:S(2)}) collective-permute-start(bf16[192,512]{1,0:T(8,128)(2,1)S(1)} %bitcast.74), channel_id=1, source_target_pairs={{0,6},{1,7},{2,0},{3,1},{4,2},{5,3},{6,4},{7,5},{8,14},{9,15},{10,... | collective-permute-start | bytes 589832 | tf_op jit(solution)/shard_map/ppermute | solution.py:33
  152.5 4.0 %collective-permute-start.2 = (bf16[192,512]{1,0:T(8,128)(2,1)S(1)}, bf16[192,512]{1,0:T(8,128)(2,1)S(1)}, u32[]{:S(2)}, u32[]{:S(2)}) collective-permute-start(bf16[192,512]{1,0:T(8,128)(2,1)S(1)} %bitcast.72), channel_id=1, source_target_pairs={{0,5},{1,6},{2,7},{3,0},{4,1},{5,2},{6,3},{7,4},{8,13},{9,14},{10,... | collective-permute-start | bytes 589832 | tf_op jit(solution)/shard_map/ppermute | solution.py:33
  156.5 4.3 %collective-permute-start.3 = (bf16[192,512]{1,0:T(8,128)(2,1)S(1)}, bf16[192,512]{1,0:T(8,128)(2,1)S(1)}, u32[]{:S(2)}, u32[]{:S(2)}) collective-permute-start(bf16[192,512]{1,0:T(8,128)(2,1)S(1)} %bitcast.71), channel_id=1, source_target_pairs={{0,4},{1,5},{2,6},{3,7},{4,0},{5,1},{6,2},{7,3},{8,12},{9,13},{10,... | collective-permute-start | bytes 589832 | tf_op jit(solution)/shard_map/ppermute | solution.py:33
  160.9 2.8 %collective-permute-start.4 = (bf16[192,512]{1,0:T(8,128)(2,1)S(1)}, bf16[192,512]{1,0:T(8,128)(2,1)S(1)}, u32[]{:S(2)}, u32[]{:S(2)}) collective-permute-start(bf16[192,512]{1,0:T(8,128)(2,1)S(1)} %bitcast.70), channel_id=1, source_target_pairs={{0,3},{1,4},{2,5},{3,6},{4,7},{5,0},{6,1},{7,2},{8,11},{9,12},{10,... | collective-permute-start | bytes 589832 | tf_op jit(solution)/shard_map/ppermute | solution.py:33
  163.6 0.7 bitcast_dynamic-update-slice_fusion
  164.4 0.0 collective-permute-done
  164.4 5.5 %collective-permute-start.5 = (bf16[192,512]{1,0:T(8,128)(2,1)S(1)}, bf16[192,512]{1,0:T(8,128)(2,1)S(1)}, u32[]{:S(2)}, u32[]{:S(2)}) collective-permute-start(bf16[192,512]{1,0:T(8,128)(2,1)S(1)} %bitcast.73), channel_id=1, source_target_pairs={{0,2},{1,3},{2,4},{3,5},{4,6},{5,7},{6,0},{7,1},{8,10},{9,11},{10,... | collective-permute-start | bytes 589832 | tf_op jit(solution)/shard_map/ppermute | solution.py:33
  169.9 0.7 constant_dynamic-update-slice_fusion.6
  170.6 0.0 collective-permute-done.1
  170.6 2.1 collective-permute-start.6
  172.7 0.7 constant_dynamic-update-slice_fusion.5
  173.4 7.2 %collective-permute-done.2 = bf16[192,512]{1,0:T(8,128)(2,1)S(1)} collective-permute-done((bf16[192,512]{1,0:T(8,128)(2,1)S(1)}, bf16[192,512]{1,0:T(8,128)(2,1)S(1)}, u32[]{:S(2)}, u32[]{:S(2)}) %collective-permute-start.2) | collective-permute-done | bytes 196640 | tf_op jit(solution)/shard_map/ppermute | solution.py:33
  180.6 0.7 constant_dynamic-update-slice_fusion.4
  181.3 0.0 collective-permute-done.3
  181.3 0.7 constant_dynamic-update-slice_fusion.3
  182.0 7.5 %collective-permute-done.4 = bf16[192,512]{1,0:T(8,128)(2,1)S(1)} collective-permute-done((bf16[192,512]{1,0:T(8,128)(2,1)S(1)}, bf16[192,512]{1,0:T(8,128)(2,1)S(1)}, u32[]{:S(2)}, u32[]{:S(2)}) %collective-permute-start.4) | collective-permute-done | bytes 196640 | tf_op jit(solution)/shard_map/ppermute | solution.py:33
  189.5 0.7 constant_dynamic-update-slice_fusion.2
  190.2 11.3 %collective-permute-done.5 = bf16[192,512]{1,0:T(8,128)(2,1)S(1)} collective-permute-done((bf16[192,512]{1,0:T(8,128)(2,1)S(1)}, bf16[192,512]{1,0:T(8,128)(2,1)S(1)}, u32[]{:S(2)}, u32[]{:S(2)}) %collective-permute-start.5) | collective-permute-done | bytes 196640 | tf_op jit(solution)/shard_map/ppermute | solution.py:33
  201.5 0.7 constant_dynamic-update-slice_fusion.1
  202.2 8.3 %collective-permute-done.6 = bf16[192,512]{1,0:T(8,128)(2,1)S(1)} collective-permute-done((bf16[192,512]{1,0:T(8,128)(2,1)S(1)}, bf16[192,512]{1,0:T(8,128)(2,1)S(1)}, u32[]{:S(2)}, u32[]{:S(2)}) %collective-permute-start.6) | collective-permute-done | bytes 196640 | tf_op jit(solution)/shard_map/ppermute | solution.py:33
  210.5 0.7 constant_dynamic-update-slice_fusion
  211.2 2.7 %all-gather.5.cloned.1.call-done = bf16[768,1536]{0,1:T(8,128)(2,1)} async-done(((bf16[768,192]{0,1:T(8,128)(2,1)}), bf16[768,1536]{0,1:T(8,128)(2,1)}) %all-gather.5.cloned.1.call-update) | async-done | bytes 2359312 | tf_op jit(solution)/shard_map/all_gather | solution.py:57
  213.9 2.5 fusion
  216.4 2.8 %convolution_convert_fusion.1 = bf16[768,512]{1,0:T(8,128)(2,1)S(1)} fusion(bf16[768,1536]{0,1:T(8,128)(2,1)S(1)} %bitcast.67, bf16[1536,512]{1,0:T(8,128)(2,1)} %constant_dynamic-update-slice_fusion), kind=kOutput, calls=%fused_computation.14 | convolution fusion | flops 1208352768 | bytes 4718592 | tf_op jit(solution)/shard_map/dot_general | solution.py:62
  219.2 0.0 copy-start.1
  219.3 1.1 reshape.47
  220.4 11.4 %all-to-all-start.1 = ((bf16[64,12,512]{2,1,0:T(8,128)(2,1)}), bf16[64,12,512]{2,1,0:T(8,128)(2,1)S(1)}, u32[]{:S(2)}, u32[]{:S(2)}) async-start(bf16[64,12,512]{2,1,0:T(8,128)(2,1)} %reshape.47), calls=%async_computation.1 | async-start | bytes 2097152 | tf_op jit(solution)/shard_map/all_to_all | solution.py:63
  231.8 0.0 copy-done.1
  231.8 0.1 copy.102
  231.9 0.6 select_reduce_fusion
  232.5 27.9 %all-to-all-done.1 = bf16[64,12,512]{2,1,0:T(8,128)(2,1)S(1)} async-done(((bf16[64,12,512]{2,1,0:T(8,128)(2,1)}), bf16[64,12,512]{2,1,0:T(8,128)(2,1)S(1)}, u32[]{:S(2)}, u32[]{:S(2)}) %all-to-all-start.1) | async-done | bytes 786464 | tf_op jit(solution)/shard_map/all_to_all | solution.py:63
  260.3 0.2 reshape.48
  260.5 0.9 convolution_convert_fusion.2
  (11 shorter events, 0.3 us)
Async XLA Ops:
  6.5 124.6 %copy-start = (bf16[1,192,4096]{2,1,0:T(8,128)(2,1)S(1)}, bf16[1,192,4096]{2,1,0:T(8,128)(2,1)}, u32[]{:S(2)}) copy-start(bf16[1,192,4096]{2,1,0:T(8,128)(2,1)} %param.7) | copy-start | bytes 4718596
  6.5 124.6 %all-gather.3.cloned.1.call-start = ((), (), s32[]{:S(2)}) async-start(), calls=%async_computation.2 | async-start | bytes 7077888 | tf_op jit(solution)/shard_map/all_gather | solution.py:48
  57.5 78.7 %copy-start.3 = (bf16[1,192,4096]{2,1,0:T(8,128)(2,1)S(1)}, bf16[1,192,4096]{2,1,0:T(8,128)(2,1)}, u32[]{:S(2)}) copy-start(bf16[1,192,4096]{2,1,0:T(8,128)(2,1)} %param.8) | copy-start | bytes 4718596
  57.5 156.4 %all-gather.5.cloned.1.call-start = ((), (), s32[]{:S(2)}) async-start(), calls=%async_computation.3 | async-start | bytes 2654208 | tf_op jit(solution)/shard_map/all_gather | solution.py:57
  131.1 5.2 %copy-start.2 = (bf16[768,4096]{1,0:T(8,128)(2,1)S(1)}, bf16[768,4096]{1,0:T(8,128)(2,1)}, u32[]{:S(2)}) copy-start(bf16[768,4096]{1,0:T(8,128)(2,1)} %all-gather.3.cloned.1.call-done) | copy-start | bytes 18874372
  145.3 19.1 %collective-permute-start = (bf16[192,512]{1,0:T(8,128)(2,1)S(1)}, bf16[192,512]{1,0:T(8,128)(2,1)S(1)}, u32[]{:S(2)}, u32[]{:S(2)}) collective-permute-start(bf16[192,512]{1,0:T(8,128)(2,1)S(1)} %bitcast.75), channel_id=1, source_target_pairs={{0,7},{1,0},{2,1},{3,2},{4,3},{5,4},{6,5},{7,6},{8,15},{9,8},{10,9... | collective-permute-start | bytes 589832 | tf_op jit(solution)/shard_map/ppermute | solution.py:33
  148.5 22.1 %collective-permute-start.1 = (bf16[192,512]{1,0:T(8,128)(2,1)S(1)}, bf16[192,512]{1,0:T(8,128)(2,1)S(1)}, u32[]{:S(2)}, u32[]{:S(2)}) collective-permute-start(bf16[192,512]{1,0:T(8,128)(2,1)S(1)} %bitcast.74), channel_id=1, source_target_pairs={{0,6},{1,7},{2,0},{3,1},{4,2},{5,3},{6,4},{7,5},{8,14},{9,15},{10,... | collective-permute-start | bytes 589832 | tf_op jit(solution)/shard_map/ppermute | solution.py:33
  152.5 28.2 %collective-permute-start.2 = (bf16[192,512]{1,0:T(8,128)(2,1)S(1)}, bf16[192,512]{1,0:T(8,128)(2,1)S(1)}, u32[]{:S(2)}, u32[]{:S(2)}) collective-permute-start(bf16[192,512]{1,0:T(8,128)(2,1)S(1)} %bitcast.72), channel_id=1, source_target_pairs={{0,5},{1,6},{2,7},{3,0},{4,1},{5,2},{6,3},{7,4},{8,13},{9,14},{10,... | collective-permute-start | bytes 589832 | tf_op jit(solution)/shard_map/ppermute | solution.py:33
  156.5 24.8 %collective-permute-start.3 = (bf16[192,512]{1,0:T(8,128)(2,1)S(1)}, bf16[192,512]{1,0:T(8,128)(2,1)S(1)}, u32[]{:S(2)}, u32[]{:S(2)}) collective-permute-start(bf16[192,512]{1,0:T(8,128)(2,1)S(1)} %bitcast.71), channel_id=1, source_target_pairs={{0,4},{1,5},{2,6},{3,7},{4,0},{5,1},{6,2},{7,3},{8,12},{9,13},{10,... | collective-permute-start | bytes 589832 | tf_op jit(solution)/shard_map/ppermute | solution.py:33
  160.9 28.6 %collective-permute-start.4 = (bf16[192,512]{1,0:T(8,128)(2,1)S(1)}, bf16[192,512]{1,0:T(8,128)(2,1)S(1)}, u32[]{:S(2)}, u32[]{:S(2)}) collective-permute-start(bf16[192,512]{1,0:T(8,128)(2,1)S(1)} %bitcast.70), channel_id=1, source_target_pairs={{0,3},{1,4},{2,5},{3,6},{4,7},{5,0},{6,1},{7,2},{8,11},{9,12},{10,... | collective-permute-start | bytes 589832 | tf_op jit(solution)/shard_map/ppermute | solution.py:33
  164.4 37.1 %collective-permute-start.5 = (bf16[192,512]{1,0:T(8,128)(2,1)S(1)}, bf16[192,512]{1,0:T(8,128)(2,1)S(1)}, u32[]{:S(2)}, u32[]{:S(2)}) collective-permute-start(bf16[192,512]{1,0:T(8,128)(2,1)S(1)} %bitcast.73), channel_id=1, source_target_pairs={{0,2},{1,3},{2,4},{3,5},{4,6},{5,7},{6,0},{7,1},{8,10},{9,11},{10,... | collective-permute-start | bytes 589832 | tf_op jit(solution)/shard_map/ppermute | solution.py:33
  170.6 39.9 %collective-permute-start.6 = (bf16[192,512]{1,0:T(8,128)(2,1)S(1)}, bf16[192,512]{1,0:T(8,128)(2,1)S(1)}, u32[]{:S(2)}, u32[]{:S(2)}) collective-permute-start(bf16[192,512]{1,0:T(8,128)(2,1)S(1)} %bitcast.69), channel_id=1, source_target_pairs={{0,1},{1,2},{2,3},{3,4},{4,5},{5,6},{6,7},{7,0},{8,9},{9,10},{10,1... | collective-permute-start | bytes 589832 | tf_op jit(solution)/shard_map/ppermute | solution.py:33
  219.2 12.6 %copy-start.1 = (bf16[64,8]{0,1:T(8,128)(2,1)S(1)}, bf16[64,8]{0,1:T(8,128)(2,1)}, u32[]{:S(2)}) copy-start(bf16[64,8]{0,1:T(8,128)(2,1)} %param.11) | copy-start | bytes 3076
  220.4 39.9 %all-to-all-start.1 = ((bf16[64,12,512]{2,1,0:T(8,128)(2,1)}), bf16[64,12,512]{2,1,0:T(8,128)(2,1)S(1)}, u32[]{:S(2)}, u32[]{:S(2)}) async-start(bf16[64,12,512]{2,1,0:T(8,128)(2,1)} %reshape.47), calls=%async_computation.1 | async-start | bytes 2097152 | tf_op jit(solution)/shard_map/all_to_all | solution.py:63
Sparse Core Ops, SparseCore 0:
  57.6 73.4 all-gather.2
  139.4 74.5 all-gather.4
